TPU v7x, 32 devices: a whole 2x2x4 slice. The times are simulated.
32 devices in a mesh: seq: 8 (over z, core), tp: 4 (over y, x).
Axes of the slice: x: 2, y: 2, z: 4, core: 2. Of those that a mesh axis runs over, the one named last changes fastest.
Arguments:
- tokens: bfloat16 [8, 512, 2048], P('seq', None, 'tp'), may hold values from -6 to 6
- segment_ids: int32 [8, 512], P('seq'), may hold values from 0 to 15, as said below
- shard_map: int32 [32], replicated, may hold values from 0 to 31, each once
- trainer_qkv: float32 [2, 2048, 6144], P(None, ('seq', 'tp')), may hold values from -0.125 to 0.125
- trainer_up: float32 [2, 2048, 8192], P(None, ('seq', 'tp')), may hold values from -0.125 to 0.125
- qkv_bias: bfloat16 [2, 6144], P(None, 'tp'), may hold values from -4 to 4
- up_bias: bfloat16 [2, 8192], P(None, 'tp'), may hold values from -3 to 3
- dense_w: bfloat16 [2, 2048, 2048], P(None, 'tp'), may hold values from -0.125 to 0.125
- down_w: bfloat16 [2, 8192, 2048], P(None, 'tp'), may hold values from -0.0625 to 0.0625
- out_bias: float32 [2, 2048], P(None, 'tp'), may hold values from -3 to 3
- norm_gain: float32 [2, 2, 2048], replicated, may hold values from 0.1 to 1.9
- norm_shift: float32 [2, 2, 2048], replicated, may hold values from -3 to 3
Outputs:
- result: bfloat16 [8, 512, 2048], P('seq', None, 'tp')
Inputs may be any that keep to these rules, and one draw needn't show every extreme that they name: `shard_map`: each trainer shard number appears exactly once. `segment_ids`: along a row the numbers start at 0 and rise by 0 or 1 from token to token; a row holds one prompt of 512 tokens or several packed prompts.
All inputs are finite; a program needn't handle non-finite values.
Results may differ from a plain program's by a relative error of at most 0.015.
Values may be sent and summed in bfloat16 or wider, within the bound.
No kernel may reach another device: no remote copies, remote signals or barrier semaphores. Data moves between devices by JAX's collectives and lax.ppermute only.
A program may use at most 192 MiB of HBM per device.

v0:
```python
import jax
import jax.numpy as jnp
from jax import lax
from jax.sharding import PartitionSpec as P

HD = 256
ROT = 64
LAYERS = 2


def layer_norm(values, gain, shift):
    mean = jnp.mean(values, axis=-1, keepdims=True)
    centred = values - mean
    var = jnp.mean(centred * centred, axis=-1, keepdims=True)
    return centred * lax.rsqrt(var + 1e-05) * gain + shift


def positions(segs):
    length = segs.shape[-1]
    index = jnp.broadcast_to(jnp.arange(length, dtype=jnp.int32), segs.shape)
    first = jnp.ones(segs.shape[:-1] + (1,), dtype=bool)
    flag = jnp.concatenate([first, segs[..., 1:] != segs[..., :-1]], axis=-1)
    start = lax.cummax(jnp.where(flag, index, 0), axis=segs.ndim - 1)
    return index - start


def rotate(values, pos):
    half = ROT // 2
    inverse = 10000.0 ** (-(jnp.arange(half, dtype=jnp.float32) * 2.0 / ROT))
    angle = pos[..., None].astype(jnp.float32) * inverse
    cosine = jnp.cos(angle)[..., None, :]
    sine = jnp.sin(angle)[..., None, :]
    first = values[..., :half]
    second = values[..., half:ROT]
    return jnp.concatenate(
        [first * cosine - second * sine, second * cosine + first * sine, values[..., ROT:]], axis=-1
    )


def shards(
    tokens,
    segment_ids,
    shard_map,
    trainer_qkv,
    trainer_up,
    qkv_bias,
    up_bias,
    dense_w,
    down_w,
    out_bias,
    norm_gain,
    norm_shift,
):
    n_tp = lax.axis_size("tp")
    rows, length, _ = tokens.shape
    block = trainer_qkv.shape[1]
    full_width = block * n_tp * lax.axis_size("seq")
    n_blocks = full_width // block
    heads_here = qkv_bias.shape[1] // (3 * HD)
    qkv_cols = qkv_bias.shape[1]
    wq = trainer_qkv.astype(jnp.bfloat16).reshape(LAYERS, block, n_tp, qkv_cols)
    wu = trainer_up.astype(jnp.bfloat16).reshape(LAYERS, block, n_tp, up_bias.shape[1])
    width_here = tokens.shape[2]

    def exchange(x):
        return lax.all_to_all(x, "tp", split_axis=0, concat_axis=0, tiled=True)

    def spread(local):
        return jnp.broadcast_to(
            local.reshape(1, rows * length, width_here), (n_tp, rows * length, width_here)
        )

    def joined(got):
        return got.transpose(1, 0, 2).reshape(rows, length, n_tp * width_here)

    gathered = []
    for layer in range(LAYERS):
        parts = []
        for part in (wq[layer], wu[layer]):
            part = lax.all_to_all(part, "tp", split_axis=1, concat_axis=0, tiled=True)
            parts.append(lax.all_gather(part.reshape(n_tp * block, -1), "seq", axis=0, tiled=True))
        gathered.append(parts)
    whole = joined(exchange(spread(tokens)))
    pos = positions(segment_ids)
    index = jnp.arange(length, dtype=jnp.int32)
    mask = (index[None, :] <= index[:, None])[None] & (
        segment_ids[:, :, None] == segment_ids[:, None, :]
    )
    mask = mask[:, None]
    stream = tokens
    for layer in range(LAYERS):
        qkv_mat, up_mat = gathered[layer]
        if layer > 0:
            whole = joined(exchange(spread(stream)))
        permuted = jnp.take(whole.reshape(rows, length, n_blocks, block), shard_map, axis=2)
        permuted = permuted.reshape(rows * length, full_width).astype(jnp.float32)

        def norm_of(i):
            gain = jnp.take(norm_gain[layer, i].reshape(n_blocks, block), shard_map, axis=0)
            shift = jnp.take(norm_shift[layer, i].reshape(n_blocks, block), shard_map, axis=0)
            return layer_norm(permuted, gain.reshape(-1), shift.reshape(-1)).astype(jnp.bfloat16)

        attn_in = norm_of(0)
        mlp_in = norm_of(1)
        qkv = jnp.dot(attn_in, qkv_mat, preferred_element_type=jnp.float32) + qkv_bias[
            layer
        ].astype(jnp.float32)
        qkv = qkv.reshape(rows, length, heads_here, 3, HD)
        query = rotate(qkv[:, :, :, 0], pos).astype(jnp.bfloat16)
        keys = rotate(qkv[:, :, :, 1], pos).astype(jnp.bfloat16)
        vals = qkv[:, :, :, 2].astype(jnp.bfloat16)
        scores = jnp.einsum(
            "rqhd,rkhd->rhqk", query, keys, preferred_element_type=jnp.float32
        ) / jnp.sqrt(jnp.float32(HD))
        scores = jnp.where(mask, scores, -jnp.inf)
        probs = jax.nn.softmax(scores, axis=-1).astype(jnp.bfloat16)
        ctx = jnp.einsum("rhqk,rkhd->rqhd", probs, vals, preferred_element_type=jnp.float32).astype(
            jnp.bfloat16
        )
        ctx = ctx.reshape(rows * length, heads_here * HD)
        up = jnp.dot(mlp_in, up_mat, preferred_element_type=jnp.float32) + up_bias[layer].astype(
            jnp.float32
        )
        hidden_units = jax.nn.gelu(up, approximate=False).astype(jnp.bfloat16)
        partial_terms = jnp.dot(ctx, dense_w[layer], preferred_element_type=jnp.float32) + jnp.dot(
            hidden_units, down_w[layer], preferred_element_type=jnp.float32
        )
        partial_terms = partial_terms.astype(jnp.bfloat16)
        split = partial_terms.reshape(rows * length, n_tp, width_here).transpose(1, 0, 2)
        summed = jnp.sum(exchange(split).astype(jnp.float32), axis=0)
        flat_stream = stream.astype(jnp.float32).reshape(rows * length, -1)
        stream = (
            (flat_stream + summed + out_bias[layer]).astype(jnp.bfloat16).reshape(rows, length, -1)
        )
    return stream


def solution(mesh):
    in_specs = (
        P("seq", None, "tp"),
        P("seq", None),
        P(),
        P(None, ("seq", "tp"), None),
        P(None, ("seq", "tp"), None),
        P(None, "tp"),
        P(None, "tp"),
        P(None, "tp", None),
        P(None, "tp", None),
        P(None, "tp"),
        P(),
        P(),
    )
    out_specs = P("seq", None, "tp")
    return jax.shard_map(shards, mesh=mesh, in_specs=in_specs, out_specs=out_specs, check_vma=False)
```

profile of v0, /device:TPU:0, one launch (start us, length us, event | category | flops | bytes accessed | tf_op | source)
XLA Modules:
  0.0 388.9 jit_solution(17570129192269081183)
XLA Ops:
  6.5 2.1 convert_element_type.153
  8.6 1.0 fusion.184
  10.4 16.4 %all_to_all.80 = bf16[64,4,1536]{2,0,1:T(8,128)(2,1)} all-to-all(bf16[64,4,1536]{2,0,1:T(8,128)(2,1)S(1)} %copy.48), channel_id=1, replica_groups=mesh['seq'=8,'tp'=4] {'tp'}, dimensions={1} | all-to-all | bytes 1572864 | tf_op jit(solution)/shard_map/all_to_all | solution.py:80
  26.8 2.4 convert_element_type.161
  29.5 0.8 squeeze.46
  30.3 0.6 copy.54
  30.9 16.0 %all_to_all.81 = bf16[64,4,2048]{2,0,1:T(8,128)(2,1)} all-to-all(bf16[64,4,2048]{2,0,1:T(8,128)(2,1)S(1)} %copy.54), channel_id=1, replica_groups=mesh['seq'=8,'tp'=4] {'tp'}, dimensions={1} | all-to-all | bytes 2097152 | tf_op jit(solution)/shard_map/all_to_all | solution.py:80
  47.0 0.6 squeeze.48
  47.7 12.1 %all_to_all.82 = bf16[64,4,1536]{2,0,1:T(8,128)(2,1)} all-to-all(bf16[64,4,1536]{2,0,1:T(8,128)(2,1)S(1)} %copy.57), channel_id=1, replica_groups=mesh['seq'=8,'tp'=4] {'tp'}, dimensions={1} | all-to-all | bytes 1572864 | tf_op jit(solution)/shard_map/all_to_all | solution.py:80
  59.8 0.8 squeeze.52
  60.6 1.6 copy.63
  62.2 3.5 all-to-all-start.6
  66.1 0.6 gather_fusion.1
  71.5 1.3 copy.47
  73.6 2.1 all-to-all-done.6
  75.7 1.6 broadcast_in_dim.47
  77.4 3.6 all-to-all-start
  81.5 0.9 fusion.44
  82.4 1.7 multiply_cosine_fusion
  84.2 17.2 %all-to-all-done = bf16[4,512,512]{1,2,0:T(8,128)(2,1)S(1)} async-done(((bf16[4,512,512]{1,2,0:T(8,128)(2,1)}), bf16[4,512,512]{1,2,0:T(8,128)(2,1)S(1)}, u32[]{:S(2)}, u32[]{:S(2)}) %all-to-all-start) | async-done | bytes 2097184 | tf_op jit(solution)/shard_map/all_to_all | solution.py:66
  101.3 1.4 copy-done
  102.7 2.3 gather_fusion
  105.0 0.7 convert_reduce_fusion.2
  105.7 0.9 multiply_reduce_fusion.1
  106.7 2.8 add_convert_fusion.5
  109.4 8.6 %convolution_add_fusion.1 = f32[512,1536]{1,0:T(8,128)} fusion(bf16[512,2048]{0,1:T(8,128)(2,1)} %get-tuple-element.23, bf16[2048,1536]{1,0:T(8,128)(2,1)} %all-gather.5.cloned.1.call-done, f32[1536]{0:T(1024)S(1)} %get-tuple-element.16), kind=kOutput, calls=%fused_computation.73 | convolution fusion | flops 3222011904 | bytes 11540480 | tf_op jit(solution)/shard_map/dot_general | solution.py:105
  118.1 2.9 copy.49
  121.0 1.5 fusion.182
  122.5 2.6 copy.67
  125.1 2.5 copy.68
  127.6 2.3 fusion.47
  130.0 2.3 fusion.48
  132.2 3.1 fusion.79
  135.3 4.4 %fusion.186 = (f32[2,512]{1,0:T(2,128)S(1)}, f32[2,512,512]{1,2,0:T(8,128)}) fusion(pred[512,512]{0,1:T(8,128)(4,1)} %fusion.44, bf16[512,2,192]{2,0,1:T(8,128)(2,1)} %fusion.48, bf16[512,2,32]{2,0,1:T(8,128)(2,1)} %get-tuple-element.34, bf16[512,2,32]{2,0,1:T(8,128)(2,1)} %get-tuple-element.33, bf16[512,2,192]{2,0,1:T(8,128)(2,1)} %fusion.47, ...), kind=kOutput, calls=%fused_computation.267 | convolution fusion | flops 273678848 | bytes 3411968 | tf_op jit(solution)/shard_map/sub | solution.py:116
  139.7 2.9 convolution_convert_fusion.1
  142.6 31.1 %all-gather.7.cloned.1.call-done = bf16[2048,2048]{1,0:T(8,128)(2,1)} async-done(((bf16[256,2048]{1,0:T(8,128)(2,1)}), bf16[2048,2048]{1,0:T(8,128)(2,1)}) %all-gather.7.cloned.1.call-update) | async-done | bytes 8388624 | tf_op jit(solution)/shard_map/all_gather | solution.py:81
  173.8 26.3 %fusion.4 = f32[512,2048]{1,0:T(8,128)} fusion(bf16[2,2048,2048]{2,1,0:T(8,128)(2,1)} %param.24, bf16[512,2048]{0,1:T(8,128)(2,1)} %get-tuple-element.24, bf16[2048,2048]{1,0:T(8,128)(2,1)} %all-gather.7.cloned.1.call-done, f32[2048]{0:T(1024)S(1)} %bitcast.214), kind=kOutput, calls=%fused_computation.14 | convolution fusion | flops 8659140608 | bytes 23076864 | tf_op jit(solution)/shard_map/dot_general | solution.py:125
  200.1 4.2 %add_convert_fusion.3 = bf16[512,2048]{1,0:T(8,128)(2,1)S(1)} fusion(f32[512,2048]{1,0:T(8,128)} %fusion.4, bf16[512,512]{0,1:T(8,128)(2,1)S(1)} %bitcast.208, bf16[2,512,2048]{2,1,0:T(8,128)(2,1)} %param.23), kind=kOutput, calls=%fused_computation.49 | convolution fusion | flops 1075838976 | bytes 8912896 | tf_op jit(solution)/shard_map/dot_general | solution.py:125
  204.3 1.6 copy.86
  205.8 3.8 all-to-all-start.3
  209.7 25.4 %all-to-all-done.3 = bf16[4,512,512]{2,1,0:T(8,128)(2,1)S(1)} async-done(((bf16[4,512,512]{2,1,0:T(8,128)(2,1)}), bf16[4,512,512]{2,1,0:T(8,128)(2,1)S(1)}, u32[]{:S(2)}, u32[]{:S(2)}) %all-to-all-start.3) | async-done | bytes 2097184 | tf_op jit(solution)/shard_map/all_to_all | solution.py:66
  235.8 1.6 broadcast_in_dim.52
  237.4 3.6 all-to-all-start.4
  241.3 24.4 %all-to-all-done.4 = bf16[4,512,512]{1,2,0:T(8,128)(2,1)S(1)} async-done(((bf16[4,512,512]{1,2,0:T(8,128)(2,1)}), bf16[4,512,512]{1,2,0:T(8,128)(2,1)S(1)}, u32[]{:S(2)}, u32[]{:S(2)}) %all-to-all-start.4) | async-done | bytes 2097184 | tf_op jit(solution)/shard_map/all_to_all | solution.py:66
  265.6 1.4 copy-done.1
  267.0 2.3 gather_fusion.5
  269.3 0.7 convert_reduce_fusion.3
  270.1 0.9 multiply_reduce_fusion
  271.0 2.8 add_convert_fusion.2
  273.8 8.8 %convolution_add_fusion = f32[512,1536]{1,0:T(8,128)} fusion(bf16[512,2048]{0,1:T(8,128)(2,1)} %get-tuple-element.21, bf16[2048,1536]{1,0:T(8,128)(2,1)} %all-gather.9.cloned.1.call-done, f32[1536]{0:T(1024)S(1)} %get-tuple-element.15), kind=kOutput, calls=%fused_computation.72 | convolution fusion | flops 3222011904 | bytes 11540480 | tf_op jit(solution)/shard_map/dot_general | solution.py:105
  282.5 2.8 copy.58
  285.3 1.5 fusion.181
  286.8 2.6 copy.69
  289.5 2.5 copy.70
  292.0 2.3 fusion.49
  294.3 2.2 fusion.50
  296.5 3.2 fusion.83
  299.7 4.5 %fusion.191 = (f32[2,512]{1,0:T(2,128)S(1)}, f32[2,512,512]{1,2,0:T(8,128)}) fusion(pred[512,512]{0,1:T(8,128)(4,1)} %fusion.44, bf16[512,2,192]{2,0,1:T(8,128)(2,1)} %fusion.50, bf16[512,2,32]{2,0,1:T(8,128)(2,1)} %get-tuple-element.28, bf16[512,2,32]{2,0,1:T(8,128)(2,1)} %get-tuple-element.27, bf16[512,2,192]{2,0,1:T(8,128)(2,1)} %fusion.49, ...), kind=kOutput, calls=%fused_computation.268 | convolution fusion | flops 273678848 | bytes 3411968 | tf_op jit(solution)/shard_map/sub | solution.py:116
  304.2 2.9 convolution_convert_fusion
  307.0 13.9 %all-gather.11.cloned.1.call-done = bf16[2048,2048]{1,0:T(8,128)(2,1)} async-done(((bf16[256,2048]{1,0:T(8,128)(2,1)}), bf16[2048,2048]{1,0:T(8,128)(2,1)}) %all-gather.11.cloned.1.call-update) | async-done | bytes 8388624 | tf_op jit(solution)/shard_map/all_gather | solution.py:81
  321.0 26.2 %fusion.2 = f32[512,2048]{1,0:T(8,128)} fusion(bf16[2,2048,2048]{2,1,0:T(8,128)(2,1)} %param.24, bf16[512,2048]{0,1:T(8,128)(2,1)} %get-tuple-element.22, bf16[2048,2048]{1,0:T(8,128)(2,1)} %all-gather.11.cloned.1.call-done, f32[2048]{0:T(1024)S(1)} %bitcast.213), kind=kOutput, calls=%fused_computation.12 | convolution fusion | flops 8659140608 | bytes 23076864 | tf_op jit(solution)/shard_map/dot_general | solution.py:125
  347.2 4.1 %add_convert_fusion = bf16[512,2048]{1,0:T(8,128)(2,1)S(1)} fusion(f32[512,2048]{1,0:T(8,128)} %fusion.2, bf16[512,512]{0,1:T(8,128)(2,1)S(1)} %bitcast.207, bf16[2,512,2048]{2,1,0:T(8,128)(2,1)} %param.23), kind=kOutput, calls=%fused_computation.31 | convolution fusion | flops 1075838976 | bytes 8912896 | tf_op jit(solution)/shard_map/dot_general | solution.py:125
  351.5 29.4 %all_to_all.83 = bf16[4,512,512]{2,1,0:T(8,128)(2,1)S(1)} all-to-all(bf16[4,512,512]{2,1,0:T(8,128)(2,1)S(1)} %bitcast.192), channel_id=1, replica_groups=mesh['seq'=8,'tp'=4] {'tp'}, dimensions={0} | all-to-all | bytes 4194304 | tf_op jit(solution)/shard_map/all_to_all | solution.py:66
  381.2 1.0 fusion.37
  (94 shorter events, 9.2 us)
Async XLA Ops:
  6.5 102.9 %all-gather.5.cloned.1.call-start = ((), (), s32[]{:S(2)}) async-start(), calls=%async_computation.8 | async-start | bytes 7077888 | tf_op jit(solution)/shard_map/all_gather | solution.py:81
  26.8 147.0 %all-gather.7.cloned.1.call-start = ((), (), s32[]{:S(2)}) async-start(), calls=%async_computation.9 | async-start | bytes 9437184 | tf_op jit(solution)/shard_map/all_gather | solution.py:81
  30.3 16.7 %copy-start.5 = (bf16[1,64,6144]{2,1,0:T(8,128)(2,1)S(1)}, bf16[1,64,6144]{2,1,0:T(8,128)(2,1)}, u32[]{:S(2)}) copy-start(bf16[1,64,6144]{2,1,0:T(8,128)(2,1)} %get-tuple-element.31) | copy-start | bytes 2359300
  46.9 226.8 %all-gather.9.cloned.1.call-start = ((), (), s32[]{:S(2)}) async-start(), calls=%async_computation.10 | async-start | bytes 7077888 | tf_op jit(solution)/shard_map/all_gather | solution.py:81
  47.7 18.0 %copy-start.11 = (f32[2,2,2048]{2,1,0:T(2,128)S(1)}, f32[2,2,2048]{2,1,0:T(2,128)}, u32[]{:S(2)}) copy-start(f32[2,2,2048]{2,1,0:T(2,128)} %param.27) | copy-start | bytes 98308
  47.7 18.0 %copy-start.12 = (f32[2,2,2048]{2,1,0:T(2,128)S(1)}, f32[2,2,2048]{2,1,0:T(2,128)}, u32[]{:S(2)}) copy-start(f32[2,2,2048]{2,1,0:T(2,128)} %param.26) | copy-start | bytes 98308
  47.7 18.3 %copy-start.15 = (s32[32]{0:T(128)S(1)}, s32[32]{0:T(128)}, u32[]{:S(2)}) copy-start(s32[32]{0:T(128)} %param.18) | copy-start | bytes 388
  59.8 12.9 %copy-start.9 = (s32[1,512]{1,0:T(1,128)S(1)}, s32[1,512]{1,0:T(1,128)}, u32[]{:S(2)}) copy-start(s32[1,512]{1,0:T(1,128)} %param.17) | copy-start | bytes 6148
  62.2 13.5 %all-to-all-start.6 = ((bf16[64,4,2048]{2,0,1:T(8,128)(2,1)}), bf16[64,4,2048]{2,0,1:T(8,128)(2,1)S(1)}, u32[]{:S(2)}, u32[]{:S(2)}) async-start(bf16[64,4,2048]{2,0,1:T(8,128)(2,1)} %copy.63), calls=%async_computation.6 | async-start | bytes 2097152 | tf_op jit(solution)/shard_map/all_to_all | solution.py:80
  70.5 10.8 %copy-start.13 = (bf16[2,1536]{1,0:T(2,128)(2,1)S(1)}, bf16[2,1536]{1,0:T(2,128)(2,1)}, u32[]{:S(2)}) copy-start(bf16[2,1536]{1,0:T(2,128)(2,1)} %param.21) | copy-start | bytes 18436
  71.5 12.7 %copy-start.10 = (bf16[2,2048]{1,0:T(2,128)(2,1)S(1)}, bf16[2,2048]{1,0:T(2,128)(2,1)}, u32[]{:S(2)}) copy-start(bf16[2,2048]{1,0:T(2,128)(2,1)} %param.22) | copy-start | bytes 24580
  75.7 8.4 %copy-start.4 = (bf16[64,4,2048]{2,0,1:T(8,128)(2,1)}, bf16[64,4,2048]{2,0,1:T(8,128)(2,1)S(1)}, u32[]{:S(2)}) copy-start(bf16[64,4,2048]{2,0,1:T(8,128)(2,1)S(1)} %all-to-all-done.6) | copy-start | bytes 3145732
  77.4 24.0 %all-to-all-start = ((bf16[4,512,512]{1,2,0:T(8,128)(2,1)}), bf16[4,512,512]{1,2,0:T(8,128)(2,1)S(1)}, u32[]{:S(2)}, u32[]{:S(2)}) async-start(bf16[4,512,512]{1,2,0:T(8,128)(2,1)} %broadcast_in_dim.47), calls=%async_computation | async-start | bytes 4194304 | tf_op jit(solution)/shard_map/all_to_all | solution.py:66
  81.0 240.0 %all-gather.11.cloned.1.call-start = ((), (), s32[]{:S(2)}) async-start(), calls=%async_computation.11 | async-start | bytes 9437184 | tf_op jit(solution)/shard_map/all_gather | solution.py:81
  101.3 1.4 copy-start
  173.8 26.3 %copy-start.8 = (bf16[2,256,512]{2,1,0:T(8,128)(2,1)S(1)}, bf16[2,256,512]{2,1,0:T(8,128)(2,1)}, u32[]{:S(2)}) copy-start(bf16[2,256,512]{2,1,0:T(8,128)(2,1)} %convolution_convert_fusion.1) | copy-start | bytes 1572868
  204.3 5.4 %copy-start.14 = (f32[2,512]{1,0:T(2,128)S(1)}, f32[2,512]{1,0:T(2,128)}, u32[]{:S(2)}) copy-start(f32[2,512]{1,0:T(2,128)} %param.25) | copy-start | bytes 12292
  205.8 29.6 %copy-start.6 = (bf16[1,512,512]{2,1,0:T(8,128)(2,1)S(1)}, bf16[1,512,512]{2,1,0:T(8,128)(2,1)}, u32[]{:S(2)}) copy-start(bf16[1,512,512]{2,1,0:T(8,128)(2,1)} %param.16) | copy-start | bytes 1572868
  205.8 29.2 %all-to-all-start.3 = ((bf16[4,512,512]{2,1,0:T(8,128)(2,1)}), bf16[4,512,512]{2,1,0:T(8,128)(2,1)S(1)}, u32[]{:S(2)}, u32[]{:S(2)}) async-start(bf16[4,512,512]{2,1,0:T(8,128)(2,1)} %bitcast.191), calls=%async_computation.3 | async-start | bytes 4194304 | tf_op jit(solution)/shard_map/all_to_all | solution.py:66
  235.6 1.8 copy-start.2
  237.4 28.3 %all-to-all-start.4 = ((bf16[4,512,512]{1,2,0:T(8,128)(2,1)}), bf16[4,512,512]{1,2,0:T(8,128)(2,1)S(1)}, u32[]{:S(2)}, u32[]{:S(2)}) async-start(bf16[4,512,512]{1,2,0:T(8,128)(2,1)} %broadcast_in_dim.52), calls=%async_computation.4 | async-start | bytes 4194304 | tf_op jit(solution)/shard_map/all_to_all | solution.py:66
  265.6 1.4 copy-start.1
  321.0 26.2 %copy-start.7 = (bf16[2,256,512]{2,1,0:T(8,128)(2,1)S(1)}, bf16[2,256,512]{2,1,0:T(8,128)(2,1)}, u32[]{:S(2)}) copy-start(bf16[2,256,512]{2,1,0:T(8,128)(2,1)} %convolution_convert_fusion) | copy-start | bytes 1572868
  351.5 29.8 %copy-start.3 = (bf16[1,512,512]{2,1,0:T(8,128)(2,1)S(1)}, bf16[1,512,512]{2,1,0:T(8,128)(2,1)}, u32[]{:S(2)}) copy-start(bf16[1,512,512]{2,1,0:T(8,128)(2,1)} %copy-done.2) | copy-start | bytes 1572868
Sparse Core Ops, SparseCore 0:
  26.9 64.4 all-gather.4
  93.0 80.6 all-gather.6
  175.4 63.2 all-gather.8
  240.2 80.7 all-gather.10
where the time goes:
time: 395 us; the launch traced here: 389 us
  waiting for transfers between devices  114 us (29%)
  matrix products  92.9 us (24%)
  blocking collectives  73.9 us (19%)
  local copies, waits for them, and re-layouts  54.4 us (14%)
  other arithmetic  24.9 us (6%)
  starting transfers between devices  15 us (4%)
  between operations  13.7 us (3%)
    all_to_all x3, waiting for transfers between devices, exchange(): return lax.all_to_all(x, 'tp', split_axis=0, concat_axis=0, tiled=True)  66.9 us
    dot_general x2, matrix products, shards(): jnp.dot(hidden_units, down_w[layer], preferred_element_type=jnp.float32)  52.6 us
    all_gather x4, waiting for transfers between devices, shards(): lax.all_gather(part.reshape(n_tp * block, -1), 'seq', axis=0, tiled=True)  45.1 us
    all_to_all x3, blocking collectives, shards(): part = lax.all_to_all(part, 'tp', split_axis=1, concat_axis=0, tiled=True)  44.5 us
    all_to_all x1, blocking collectives, exchange(): return lax.all_to_all(x, 'tp', split_axis=0, concat_axis=0, tiled=True)  29.4 us
    dot_general x2, matrix products, shards(): jnp.dot(attn_in, qkv_mat, preferred_element_type=jnp.float32)  17.4 us
    unnamed x36, local copies, waits for them, and re-layouts  13.1 us
    all_to_all x3, starting transfers between devices, exchange(): return lax.all_to_all(x, 'tp', split_axis=0, concat_axis=0, tiled=True)  11 us
  transfers between devices with their start and end apart: 8, of which 6 were waited for; matrix products, arithmetic and copies ran while one was open for 34% of the time, Pallas kernels for 0%

commit v1 on v0

--- a/solution.py
+++ b/solution.py
@@ -6,6 +6,28 @@
 HD = 256
 ROT = 64
 LAYERS = 2
+
+
+def laid_out(blocks, dim):
+    shape = list(blocks.shape[1:])
+    shape[dim] *= blocks.shape[0]
+    return jnp.moveaxis(blocks, 0, dim).reshape(shape)
+
+
+def collect(x, axis, dim):
+    devices = lax.axis_size(axis)
+    pairs = [(i, (i + 1) % devices) for i in range(devices)]
+    back = [(b, a) for a, b in pairs]
+    lower, upper = ([], [])
+    for lap in range(devices - 1):
+        if lap % 2 == 0:
+            lower.append(lax.ppermute(lower[-1] if lower else x, axis, pairs))
+        else:
+            upper.append(lax.ppermute(upper[-1] if upper else x, axis, back))
+    blocks = jnp.stack([*lower[::-1], x, *upper])
+    shift = lax.axis_index(axis) - len(lower)
+    blocks = blocks[(jnp.arange(devices) - shift) % devices]
+    return laid_out(blocks, dim)
 
 
 def layer_norm(values, gain, shift):
@@ -78,7 +100,7 @@
         parts = []
         for part in (wq[layer], wu[layer]):
             part = lax.all_to_all(part, "tp", split_axis=1, concat_axis=0, tiled=True)
-            parts.append(lax.all_gather(part.reshape(n_tp * block, -1), "seq", axis=0, tiled=True))
+            parts.append(collect(part.reshape(n_tp * block, -1), "seq", 0))
         gathered.append(parts)
     whole = joined(exchange(spread(tokens)))
     pos = positions(segment_ids)

time: 395 us -> 552 us (1.40)
  the two profiles are of different devices: /device:TPU:0 before, /device:TPU:24 now
where the time goes in v1:
time: 552 us; the launch traced here: 541 us
  waiting for transfers between devices  177 us (32%)
  local copies, waits for them, and re-layouts  151 us (27%)
  matrix products  90.8 us (16%)
  starting transfers between devices  67 us (12%)
  blocking collectives  28.5 us (5%)
  other arithmetic  26.7 us (5%)
    ppermute x16, waiting for transfers between devices, collect(): lower.append(lax.ppermute(lower[-1] if lower else x, axis, pairs))  82.6 us
    unnamed x86, local copies, waits for them, and re-layouts  67.9 us
    dot_general x2, matrix products, shards(): jnp.dot(hidden_units, down_w[layer], preferred_element_type=jnp.float32)  51.9 us
    ppermute x12, waiting for transfers between devices, collect(): upper.append(lax.ppermute(upper[-1] if upper else x, axis, back))  51.5 us
    ppermute x16, starting transfers between devices, collect(): lower.append(lax.ppermute(lower[-1] if lower else x, axis, pairs))  30 us
    gather x4, local copies, waits for them, and re-layouts, collect(): blocks = blocks[(jnp.arange(devices) - shift) % devices]  29.6 us
    all_to_all x3, waiting for transfers between devices, exchange(): return lax.all_to_all(x, 'tp', split_axis=0, concat_axis=0, tiled=True)  28.6 us
    all_to_all x1, blocking collectives, exchange(): return lax.all_to_all(x, 'tp', split_axis=0, concat_axis=0, tiled=True)  28.5 us
  transfers between devices with their start and end apart: 35, of which 16 were waited for; matrix products, arithmetic and copies ran while one was open for 36% of the time, Pallas kernels for 0%

profile of v1, /device:TPU:24, one launch (start us, length us, event | category | flops | bytes accessed | tf_op | source)
XLA Modules:
  0.0 541.4 jit_solution(1579487758090627688)
XLA Ops:
  4.7 4.2 all-to-all-start.1
  9.0 2.4 convert_element_type.167
  15.5 2.3 squeeze.48
  20.1 3.5 all-to-all-start.5
  24.9 9.0 %all-to-all-done.5 = bf16[64,4,1536]{2,0,1:T(8,128)(2,1)S(1)} async-done(((bf16[64,4,1536]{2,0,1:T(8,128)(2,1)}), bf16[64,4,1536]{2,0,1:T(8,128)(2,1)S(1)}, u32[]{:S(2)}, u32[]{:S(2)}) %all-to-all-start.5) | async-done | bytes 786464 | tf_op jit(solution)/shard_map/all_to_all | solution.py:102
  33.9 3.5 all-to-all-start.2
  46.5 3.9 all-to-all-done.2
  50.5 2.9 broadcast_in_dim.43
  53.4 3.6 all-to-all-start
  59.2 10.2 %collective-permute-done.1 = bf16[256,1536]{1,0:T(8,128)(2,1)} collective-permute-done((bf16[256,1536]{1,0:T(8,128)(2,1)}, bf16[256,1536]{1,0:T(8,128)(2,1)}, u32[]{:S(2)}, u32[]{:S(2)}) %collective-permute-start.1) | collective-permute-done | bytes 786464 | tf_op jit(solution)/shard_map/ppermute | solution.py:24
  75.0 3.5 collective-permute-start.7
  78.6 2.8 all-to-all-done
  81.4 4.3 all-to-all-start.6
  91.6 3.3 fusion.17
  94.9 3.8 collective-permute-done.14
  98.7 42.4 %collective-permute-done.3 = bf16[256,1536]{1,0:T(8,128)(2,1)S(1)} collective-permute-done((bf16[256,1536]{1,0:T(8,128)(2,1)}, bf16[256,1536]{1,0:T(8,128)(2,1)S(1)}, u32[]{:S(2)}, u32[]{:S(2)}) %collective-permute-start.3) | collective-permute-done | bytes 786464 | tf_op jit(solution)/shard_map/ppermute | solution.py:24
  141.1 5.7 %collective-permute-start.15 = (bf16[256,1536]{1,0:T(8,128)(2,1)}, bf16[256,1536]{1,0:T(8,128)(2,1)}, u32[]{:S(2)}, u32[]{:S(2)}) collective-permute-start(bf16[256,1536]{1,0:T(8,128)(2,1)} %collective-permute-done.14), channel_id=1, source_target_pairs={{0,4},{4,8},{8,12},{12,16},{16,20},{20,24},{24,28},{28,0},{1,5},{5... | collective-permute-start | bytes 2359304 | tf_op jit(solution)/shard_map/ppermute | solution.py:24
  154.2 4.2 collective-permute-start.21
  164.2 12.3 %collective-permute-done.21 = bf16[256,2048]{1,0:T(8,128)(2,1)} collective-permute-done((bf16[256,2048]{1,0:T(8,128)(2,1)}, bf16[256,2048]{1,0:T(8,128)(2,1)}, u32[]{:S(2)}, u32[]{:S(2)}) %collective-permute-start.21) | collective-permute-done | bytes 1048608 | tf_op jit(solution)/shard_map/ppermute | solution.py:24
  176.5 6.6 %collective-permute-start.8 = (bf16[256,2048]{1,0:T(8,128)(2,1)}, bf16[256,2048]{1,0:T(8,128)(2,1)}, u32[]{:S(2)}, u32[]{:S(2)}) collective-permute-start(bf16[256,2048]{1,0:T(8,128)(2,1)} %collective-permute-done.7), channel_id=1, source_target_pairs={{0,4},{4,8},{8,12},{12,16},{16,20},{20,24},{24,28},{28,0},{1,5},{5... | collective-permute-start | bytes 3145736 | tf_op jit(solution)/shard_map/ppermute | solution.py:24
  184.5 14.7 %collective-permute-done.19 = bf16[256,1536]{1,0:T(8,128)(2,1)S(1)} collective-permute-done((bf16[256,1536]{1,0:T(8,128)(2,1)}, bf16[256,1536]{1,0:T(8,128)(2,1)S(1)}, u32[]{:S(2)}, u32[]{:S(2)}) %collective-permute-start.19) | collective-permute-done | bytes 786464 | tf_op jit(solution)/shard_map/ppermute | solution.py:26
  199.9 16.0 %collective-permute-done.6 = bf16[256,1536]{1,0:T(8,128)(2,1)S(1)} collective-permute-done((bf16[256,1536]{1,0:T(8,128)(2,1)S(1)}, bf16[256,1536]{1,0:T(8,128)(2,1)S(1)}, u32[]{:S(2)}, u32[]{:S(2)}) %collective-permute-start.6) | collective-permute-done | bytes 786464 | tf_op jit(solution)/shard_map/ppermute | solution.py:26
  219.1 6.5 %gather_fusion = bf16[8,256,1536]{2,1,0:T(8,128)(2,1)} fusion(bf16[8,256,1536]{2,1,0:T(8,128)(2,1)} %bitcast_dynamic-update-slice_fusion.21, s32[1024]{0:T(1024)S(1)} %pad_clamp_fusion), kind=kCustom, calls=%fused_computation.10 | custom fusion | bytes 12582944 | tf_op jit(solution)/shard_map/gather | solution.py:29
  225.7 8.0 %convolution_add_fusion.1 = f32[512,1536]{1,0:T(8,128)} fusion(bf16[512,2048]{0,1:T(8,128)(2,1)S(1)} %bitcast.271, bf16[2048,1536]{1,0:T(8,128)(2,1)} %bitcast.262, f32[1536]{0:T(1024)S(1)} %copy-done.22), kind=kOutput, calls=%fused_computation.87 | convolution fusion | flops 3222011904 | bytes 11540480 | tf_op jit(solution)/shard_map/dot_general | solution.py:127
  233.7 2.4 copy.53
  240.7 20.3 %collective-permute-done.26 = bf16[256,2048]{1,0:T(8,128)(2,1)} collective-permute-done((bf16[256,2048]{1,0:T(8,128)(2,1)}, bf16[256,2048]{1,0:T(8,128)(2,1)}, u32[]{:S(2)}, u32[]{:S(2)}) %collective-permute-start.26) | collective-permute-done | bytes 1048608 | tf_op jit(solution)/shard_map/ppermute | solution.py:26
  275.9 2.6 copy.71
  280.8 2.5 copy.72
  289.8 6.4 %gather_fusion.2 = bf16[8,256,1536]{2,1,0:T(8,128)(2,1)} fusion(bf16[8,256,1536]{2,1,0:T(8,128)(2,1)} %bitcast_dynamic-update-slice_fusion.14, s32[1024]{0:T(1024)S(1)} %pad_clamp_fusion), kind=kCustom, calls=%fused_computation.12 | custom fusion | bytes 12582944 | tf_op jit(solution)/shard_map/gather | solution.py:29
  296.1 3.1 fusion.95
  299.2 4.4 fusion.204
  303.6 2.8 convolution_convert_fusion.1
  306.5 2.9 collective-permute-start.24
  309.4 13.2 %collective-permute-done.10 = bf16[256,2048]{1,0:T(8,128)(2,1)} collective-permute-done((bf16[256,2048]{1,0:T(8,128)(2,1)}, bf16[256,2048]{1,0:T(8,128)(2,1)}, u32[]{:S(2)}, u32[]{:S(2)}) %collective-permute-start.10) | collective-permute-done | bytes 1048608 | tf_op jit(solution)/shard_map/ppermute | solution.py:24
  322.6 2.4 bitcast_dynamic-update-slice_fusion.13
  327.3 2.3 bitcast_dynamic-update-slice_fusion.11
  329.6 2.3 bitcast_dynamic-update-slice_fusion.10
  333.1 2.3 bitcast_dynamic-update-slice_fusion.9
  335.4 2.3 bitcast_dynamic-update-slice_fusion.8
  340.0 8.6 %gather_fusion.1 = bf16[8,256,2048]{2,1,0:T(8,128)(2,1)} fusion(bf16[8,256,2048]{2,1,0:T(8,128)(2,1)} %bitcast_dynamic-update-slice_fusion.7, s32[1024]{0:T(1024)S(1)} %pad_clamp_fusion), kind=kCustom, calls=%fused_computation.11 | custom fusion | bytes 16777248 | tf_op jit(solution)/shard_map/gather | solution.py:29
  348.7 25.6 %fusion.4 = f32[512,2048]{1,0:T(8,128)} fusion(bf16[2,2048,2048]{2,1,0:T(8,128)(2,1)} %param.24, bf16[512,2048]{0,1:T(8,128)(2,1)S(1)} %bitcast.270, bf16[2048,2048]{1,0:T(8,128)(2,1)} %bitcast.248, f32[2048]{0:T(1024)S(1)} %bitcast.282), kind=kOutput, calls=%fused_computation.18 | convolution fusion | flops 8659140608 | bytes 23076864 | tf_op jit(solution)/shard_map/dot_general | solution.py:147
  374.2 4.3 add_convert_fusion.1
  380.0 4.2 all-to-all-start.3
  387.6 2.4 bitcast_dynamic-update-slice_fusion.4
  390.0 2.3 bitcast_dynamic-update-slice_fusion.3
  392.3 17.0 %all-to-all-done.3 = bf16[4,512,512]{2,1,0:T(8,128)(2,1)S(1)} async-done(((bf16[4,512,512]{2,1,0:T(8,128)(2,1)}), bf16[4,512,512]{2,1,0:T(8,128)(2,1)S(1)}, u32[]{:S(2)}, u32[]{:S(2)}) %all-to-all-start.3) | async-done | bytes 2097184 | tf_op jit(solution)/shard_map/all_to_all | solution.py:88
  411.6 3.6 all-to-all-start.4
  415.2 2.4 constant_dynamic-update-slice_fusion.3
  417.6 2.3 bitcast_dynamic-update-slice_fusion.2
  419.9 2.3 bitcast_dynamic-update-slice_fusion.1
  424.6 8.1 %gather_fusion.3 = bf16[8,256,2048]{2,1,0:T(8,128)(2,1)} fusion(bf16[8,256,2048]{2,1,0:T(8,128)(2,1)} %bitcast_dynamic-update-slice_fusion, s32[1024]{0:T(1024)S(1)} %pad_clamp_fusion), kind=kCustom, calls=%fused_computation.13 | custom fusion | bytes 16777248 | tf_op jit(solution)/shard_map/gather | solution.py:29
  432.6 8.8 %all-to-all-done.4 = bf16[4,512,512]{1,2,0:T(8,128)(2,1)S(1)} async-done(((bf16[4,512,512]{1,2,0:T(8,128)(2,1)}), bf16[4,512,512]{1,2,0:T(8,128)(2,1)S(1)}, u32[]{:S(2)}, u32[]{:S(2)}) %all-to-all-start.4) | async-done | bytes 2097184 | tf_op jit(solution)/shard_map/all_to_all | solution.py:88
  446.7 2.8 fusion.21
  449.5 8.0 %convolution_add_fusion = f32[512,1536]{1,0:T(8,128)} fusion(bf16[512,2048]{0,1:T(8,128)(2,1)S(1)} %bitcast.273, bf16[2048,1536]{1,0:T(8,128)(2,1)} %bitcast.261, f32[1536]{0:T(1024)S(1)} %copy-done.21), kind=kOutput, calls=%fused_computation.86 | convolution fusion | flops 3222011904 | bytes 11540480 | tf_op jit(solution)/shard_map/dot_general | solution.py:127
  457.5 2.6 copy.62
  461.6 2.6 copy.73
  464.2 2.5 copy.74
  466.8 2.3 fusion.65
  469.1 3.1 fusion.99
  473.2 4.4 fusion.209
  477.7 2.8 convolution_convert_fusion
  480.5 26.3 %fusion.2 = f32[512,2048]{1,0:T(8,128)} fusion(bf16[2,2048,2048]{2,1,0:T(8,128)(2,1)} %param.24, bf16[512,2048]{0,1:T(8,128)(2,1)} %bitcast.272, bf16[2048,2048]{1,0:T(8,128)(2,1)} %bitcast.247, f32[2048]{0:T(1024)S(1)} %bitcast.281), kind=kOutput, calls=%fused_computation.16 | convolution fusion | flops 8659140608 | bytes 23076864 | tf_op jit(solution)/shard_map/dot_general | solution.py:147
  506.9 4.1 add_convert_fusion
  511.2 28.5 %all_to_all.80 = bf16[4,512,512]{2,1,0:T(8,128)(2,1)S(1)} all-to-all(bf16[4,512,512]{2,1,0:T(8,128)(2,1)S(1)} %bitcast.252), channel_id=1, replica_groups=mesh['seq'=8,'tp'=4] {'tp'}, dimensions={0} | all-to-all | bytes 4194304 | tf_op jit(solution)/shard_map/all_to_all | solution.py:88
  (193 shorter events, 106.5 us)
Async XLA Ops:
  4.7 15.4 %all-to-all-start.1 = ((bf16[64,4,1536]{2,0,1:T(8,128)(2,1)}), bf16[64,4,1536]{2,0,1:T(8,128)(2,1)}, u32[]{:S(2)}, u32[]{:S(2)}) async-start(bf16[64,4,1536]{2,0,1:T(8,128)(2,1)} %copy.52), calls=%async_computation.1 | async-start | bytes 1572864 | tf_op jit(solution)/shard_map/all_to_all | solution.py:102
  8.9 2.7 copy-start.16
  9.0 2.7 copy-start.17
  9.0 3.0 copy-start.26
  13.1 10.5 %copy-start.14 = (s32[1,512]{1,0:T(1,128)S(1)}, s32[1,512]{1,0:T(1,128)}, u32[]{:S(2)}) copy-start(s32[1,512]{1,0:T(1,128)} %param.17) | copy-start | bytes 6148
  13.1 11.2 %copy-start.18 = (bf16[2,1536]{1,0:T(2,128)(2,1)S(1)}, bf16[2,1536]{1,0:T(2,128)(2,1)}, u32[]{:S(2)}) copy-start(bf16[2,1536]{1,0:T(2,128)(2,1)} %param.21) | copy-start | bytes 18436
  20.1 13.8 %all-to-all-start.5 = ((bf16[64,4,1536]{2,0,1:T(8,128)(2,1)}), bf16[64,4,1536]{2,0,1:T(8,128)(2,1)S(1)}, u32[]{:S(2)}, u32[]{:S(2)}) async-start(bf16[64,4,1536]{2,0,1:T(8,128)(2,1)} %copy.61), calls=%async_computation.5 | async-start | bytes 1572864 | tf_op jit(solution)/shard_map/all_to_all | solution.py:102
  24.9 21.0 %copy-start.25 = (f32[2,512]{1,0:T(2,128)S(1)}, f32[2,512]{1,0:T(2,128)}, u32[]{:S(2)}) copy-start(f32[2,512]{1,0:T(2,128)} %param.25) | copy-start | bytes 12292
  33.9 9.6 %copy-start.7 = (bf16[64,4,1536]{2,0,1:T(8,128)(2,1)}, bf16[64,4,1536]{2,0,1:T(8,128)(2,1)S(1)}, u32[]{:S(2)}) copy-start(bf16[64,4,1536]{2,0,1:T(8,128)(2,1)S(1)} %all-to-all-done.5) | copy-start | bytes 2359300
  33.9 16.6 %all-to-all-start.2 = ((bf16[64,4,2048]{2,0,1:T(8,128)(2,1)}), bf16[64,4,2048]{2,0,1:T(8,128)(2,1)S(1)}, u32[]{:S(2)}, u32[]{:S(2)}) async-start(bf16[64,4,2048]{2,0,1:T(8,128)(2,1)} %copy.58), calls=%async_computation.2 | async-start | bytes 2097152 | tf_op jit(solution)/shard_map/all_to_all | solution.py:102
  45.8 12.7 %copy-start.15 = (bf16[2,2048]{1,0:T(2,128)(2,1)S(1)}, bf16[2,2048]{1,0:T(2,128)(2,1)}, u32[]{:S(2)}) copy-start(bf16[2,2048]{1,0:T(2,128)(2,1)} %param.22) | copy-start | bytes 24580
  45.9 11.7 %collective-permute-start = (bf16[256,1536]{1,0:T(8,128)(2,1)}, bf16[256,1536]{1,0:T(8,128)(2,1)}, u32[]{:S(2)}, u32[]{:S(2)}) collective-permute-start(bf16[256,1536]{1,0:T(8,128)(2,1)} %bitcast.9), channel_id=1, source_target_pairs={{0,4},{4,8},{8,12},{12,16},{16,20},{20,24},{24,28},{28,0},{1,5},{5... | collective-permute-start | bytes 2359304 | tf_op jit(solution)/shard_map/ppermute | solution.py:24
  50.5 44.4 %copy-start.5 = (bf16[64,4,2048]{2,0,1:T(8,128)(2,1)}, bf16[64,4,2048]{2,0,1:T(8,128)(2,1)S(1)}, u32[]{:S(2)}) copy-start(bf16[64,4,2048]{2,0,1:T(8,128)(2,1)S(1)} %all-to-all-done.2) | copy-start | bytes 3145732
  53.4 28.0 %all-to-all-start = ((bf16[4,512,512]{1,2,0:T(8,128)(2,1)}), bf16[4,512,512]{1,2,0:T(8,128)(2,1)S(1)}, u32[]{:S(2)}, u32[]{:S(2)}) async-start(bf16[4,512,512]{1,2,0:T(8,128)(2,1)} %broadcast_in_dim.43), calls=%async_computation | async-start | bytes 4194304 | tf_op jit(solution)/shard_map/all_to_all | solution.py:88
  57.7 11.7 %collective-permute-start.1 = (bf16[256,1536]{1,0:T(8,128)(2,1)}, bf16[256,1536]{1,0:T(8,128)(2,1)}, u32[]{:S(2)}, u32[]{:S(2)}) collective-permute-start(bf16[256,1536]{1,0:T(8,128)(2,1)} %collective-permute-done), channel_id=1, source_target_pairs={{0,4},{4,8},{8,12},{12,16},{16,20},{20,24},{24,28},{28,0},{1,5},{5... | collective-permute-start | bytes 2359304 | tf_op jit(solution)/shard_map/ppermute | solution.py:24
  69.4 19.3 %collective-permute-start.2 = (bf16[256,1536]{1,0:T(8,128)(2,1)}, bf16[256,1536]{1,0:T(8,128)(2,1)}, u32[]{:S(2)}, u32[]{:S(2)}) collective-permute-start(bf16[256,1536]{1,0:T(8,128)(2,1)} %collective-permute-done.1), channel_id=1, source_target_pairs={{0,4},{4,8},{8,12},{12,16},{16,20},{20,24},{24,28},{28,0},{1,5},{5... | collective-permute-start | bytes 2359304 | tf_op jit(solution)/shard_map/ppermute | solution.py:24
  71.2 23.7 %collective-permute-start.4 = (bf16[256,1536]{1,0:T(8,128)(2,1)}, bf16[256,1536]{1,0:T(8,128)(2,1)}, u32[]{:S(2)}, u32[]{:S(2)}) collective-permute-start(bf16[256,1536]{1,0:T(8,128)(2,1)} %bitcast.9), channel_id=1, source_target_pairs={{4,0},{8,4},{12,8},{16,12},{20,16},{24,20},{28,24},{0,28},{5,1},{9... | collective-permute-start | bytes 2359304 | tf_op jit(solution)/shard_map/ppermute | solution.py:26
  72.9 25.8 %collective-permute-start.14 = (bf16[256,1536]{1,0:T(8,128)(2,1)}, bf16[256,1536]{1,0:T(8,128)(2,1)}, u32[]{:S(2)}, u32[]{:S(2)}) collective-permute-start(bf16[256,1536]{1,0:T(8,128)(2,1)} %bitcast.267), channel_id=1, source_target_pairs={{0,4},{4,8},{8,12},{12,16},{16,20},{20,24},{24,28},{28,0},{1,5},{5... | collective-permute-start | bytes 2359304 | tf_op jit(solution)/shard_map/ppermute | solution.py:24
  75.0 79.1 %collective-permute-start.18 = (bf16[256,1536]{1,0:T(8,128)(2,1)}, bf16[256,1536]{1,0:T(8,128)(2,1)}, u32[]{:S(2)}, u32[]{:S(2)}) collective-permute-start(bf16[256,1536]{1,0:T(8,128)(2,1)} %bitcast.268), channel_id=1, source_target_pairs={{4,0},{8,4},{12,8},{16,12},{20,16},{24,20},{28,24},{0,28},{5,1},{9... | collective-permute-start | bytes 2359304 | tf_op jit(solution)/shard_map/ppermute | solution.py:26
  75.0 83.3 %collective-permute-start.7 = (bf16[256,2048]{1,0:T(8,128)(2,1)S(1)}, bf16[256,2048]{1,0:T(8,128)(2,1)}, u32[]{:S(2)}, u32[]{:S(2)}) collective-permute-start(bf16[256,2048]{1,0:T(8,128)(2,1)S(1)} %bitcast.264), channel_id=1, source_target_pairs={{0,4},{4,8},{8,12},{12,16},{16,20},{20,24},{24,28},{28,0},{1,5},{5... | collective-permute-start | bytes 3145736 | tf_op jit(solution)/shard_map/ppermute | solution.py:24
  81.4 4.3 copy-start
  81.4 72.8 %all-to-all-start.6 = ((bf16[64,4,2048]{2,0,1:T(8,128)(2,1)}), bf16[64,4,2048]{2,0,1:T(8,128)(2,1)}, u32[]{:S(2)}, u32[]{:S(2)}) async-start(bf16[64,4,2048]{2,0,1:T(8,128)(2,1)} %copy.67), calls=%async_computation.6 | async-start | bytes 2097152 | tf_op jit(solution)/shard_map/all_to_all | solution.py:102
  88.7 52.4 %collective-permute-start.3 = (bf16[256,1536]{1,0:T(8,128)(2,1)}, bf16[256,1536]{1,0:T(8,128)(2,1)S(1)}, u32[]{:S(2)}, u32[]{:S(2)}) collective-permute-start(bf16[256,1536]{1,0:T(8,128)(2,1)} %collective-permute-done.2), channel_id=1, source_target_pairs={{0,4},{4,8},{8,12},{12,16},{16,20},{20,24},{24,28},{28,0},{1,5},{5... | collective-permute-start | bytes 2359304 | tf_op jit(solution)/shard_map/ppermute | solution.py:24
  94.9 65.5 %collective-permute-start.11 = (bf16[256,2048]{1,0:T(8,128)(2,1)S(1)}, bf16[256,2048]{1,0:T(8,128)(2,1)}, u32[]{:S(2)}, u32[]{:S(2)}) collective-permute-start(bf16[256,2048]{1,0:T(8,128)(2,1)S(1)} %bitcast.265), channel_id=1, source_target_pairs={{4,0},{8,4},{12,8},{16,12},{20,16},{24,20},{28,24},{0,28},{5,1},{9... | collective-permute-start | bytes 3145736 | tf_op jit(solution)/shard_map/ppermute | solution.py:26
  98.7 61.7 %collective-permute-start.5 = (bf16[256,1536]{1,0:T(8,128)(2,1)}, bf16[256,1536]{1,0:T(8,128)(2,1)S(1)}, u32[]{:S(2)}, u32[]{:S(2)}) collective-permute-start(bf16[256,1536]{1,0:T(8,128)(2,1)} %collective-permute-done.4), channel_id=1, source_target_pairs={{4,0},{8,4},{12,8},{16,12},{20,16},{24,20},{28,24},{0,28},{5,1},{9... | collective-permute-start | bytes 2359304 | tf_op jit(solution)/shard_map/ppermute | solution.py:26
  141.1 21.7 %collective-permute-start.15 = (bf16[256,1536]{1,0:T(8,128)(2,1)}, bf16[256,1536]{1,0:T(8,128)(2,1)}, u32[]{:S(2)}, u32[]{:S(2)}) collective-permute-start(bf16[256,1536]{1,0:T(8,128)(2,1)} %collective-permute-done.14), channel_id=1, source_target_pairs={{0,4},{4,8},{8,12},{12,16},{16,20},{20,24},{24,28},{28,0},{1,5},{5... | collective-permute-start | bytes 2359304 | tf_op jit(solution)/shard_map/ppermute | solution.py:24
  154.2 22.4 %collective-permute-start.21 = (bf16[256,2048]{1,0:T(8,128)(2,1)}, bf16[256,2048]{1,0:T(8,128)(2,1)}, u32[]{:S(2)}, u32[]{:S(2)}) collective-permute-start(bf16[256,2048]{1,0:T(8,128)(2,1)} %bitcast.98), channel_id=1, source_target_pairs={{0,4},{4,8},{8,12},{12,16},{16,20},{20,24},{24,28},{28,0},{1,5},{5... | collective-permute-start | bytes 3145736 | tf_op jit(solution)/shard_map/ppermute | solution.py:24
  158.3 24.8 %collective-permute-start.25 = (bf16[256,2048]{1,0:T(8,128)(2,1)}, bf16[256,2048]{1,0:T(8,128)(2,1)}, u32[]{:S(2)}, u32[]{:S(2)}) collective-permute-start(bf16[256,2048]{1,0:T(8,128)(2,1)} %bitcast.98), channel_id=1, source_target_pairs={{4,0},{8,4},{12,8},{16,12},{20,16},{24,20},{28,24},{0,28},{5,1},{9... | collective-permute-start | bytes 3145736 | tf_op jit(solution)/shard_map/ppermute | solution.py:26
  160.4 38.7 %collective-permute-start.19 = (bf16[256,1536]{1,0:T(8,128)(2,1)}, bf16[256,1536]{1,0:T(8,128)(2,1)S(1)}, u32[]{:S(2)}, u32[]{:S(2)}) collective-permute-start(bf16[256,1536]{1,0:T(8,128)(2,1)} %collective-permute-done.18), channel_id=1, source_target_pairs={{4,0},{8,4},{12,8},{16,12},{20,16},{24,20},{28,24},{0,28},{5,1},{9... | collective-permute-start | bytes 2359304 | tf_op jit(solution)/shard_map/ppermute | solution.py:26
  160.4 55.4 %collective-permute-start.6 = (bf16[256,1536]{1,0:T(8,128)(2,1)S(1)}, bf16[256,1536]{1,0:T(8,128)(2,1)S(1)}, u32[]{:S(2)}, u32[]{:S(2)}) collective-permute-start(bf16[256,1536]{1,0:T(8,128)(2,1)S(1)} %collective-permute-done.5), channel_id=1, source_target_pairs={{4,0},{8,4},{12,8},{16,12},{20,16},{24,20},{28,24},{0,28},{5,1},{9... | collective-permute-start | bytes 2359304 | tf_op jit(solution)/shard_map/ppermute | solution.py:26
  162.8 62.9 %collective-permute-start.16 = (bf16[256,1536]{1,0:T(8,128)(2,1)}, bf16[256,1536]{1,0:T(8,128)(2,1)}, u32[]{:S(2)}, u32[]{:S(2)}) collective-permute-start(bf16[256,1536]{1,0:T(8,128)(2,1)} %collective-permute-done.15), channel_id=1, source_target_pairs={{0,4},{4,8},{8,12},{12,16},{16,20},{20,24},{24,28},{28,0},{1,5},{5... | collective-permute-start | bytes 2359304 | tf_op jit(solution)/shard_map/ppermute | solution.py:24
  176.5 59.5 %collective-permute-start.8 = (bf16[256,2048]{1,0:T(8,128)(2,1)}, bf16[256,2048]{1,0:T(8,128)(2,1)}, u32[]{:S(2)}, u32[]{:S(2)}) collective-permute-start(bf16[256,2048]{1,0:T(8,128)(2,1)} %collective-permute-done.7), channel_id=1, source_target_pairs={{0,4},{4,8},{8,12},{12,16},{16,20},{20,24},{24,28},{28,0},{1,5},{5... | collective-permute-start | bytes 3145736 | tf_op jit(solution)/shard_map/ppermute | solution.py:24
  183.1 55.3 %collective-permute-start.12 = (bf16[256,2048]{1,0:T(8,128)(2,1)}, bf16[256,2048]{1,0:T(8,128)(2,1)}, u32[]{:S(2)}, u32[]{:S(2)}) collective-permute-start(bf16[256,2048]{1,0:T(8,128)(2,1)} %collective-permute-done.11), channel_id=1, source_target_pairs={{4,0},{8,4},{12,8},{16,12},{20,16},{24,20},{28,24},{0,28},{5,1},{9... | collective-permute-start | bytes 3145736 | tf_op jit(solution)/shard_map/ppermute | solution.py:26
  199.1 19.1 %copy-start.12 = (bf16[256,1536]{1,0:T(8,128)(2,1)}, bf16[256,1536]{1,0:T(8,128)(2,1)S(1)}, u32[]{:S(2)}) copy-start(bf16[256,1536]{1,0:T(8,128)(2,1)S(1)} %collective-permute-done.19) | copy-start | bytes 2359300
  199.1 40.2 %collective-permute-start.22 = (bf16[256,2048]{1,0:T(8,128)(2,1)}, bf16[256,2048]{1,0:T(8,128)(2,1)}, u32[]{:S(2)}, u32[]{:S(2)}) collective-permute-start(bf16[256,2048]{1,0:T(8,128)(2,1)} %collective-permute-done.21), channel_id=1, source_target_pairs={{0,4},{4,8},{8,12},{12,16},{16,20},{20,24},{24,28},{28,0},{1,5},{5... | collective-permute-start | bytes 3145736 | tf_op jit(solution)/shard_map/ppermute | solution.py:24
  215.9 45.0 %collective-permute-start.26 = (bf16[256,2048]{1,0:T(8,128)(2,1)}, bf16[256,2048]{1,0:T(8,128)(2,1)}, u32[]{:S(2)}, u32[]{:S(2)}) collective-permute-start(bf16[256,2048]{1,0:T(8,128)(2,1)} %collective-permute-done.25), channel_id=1, source_target_pairs={{4,0},{8,4},{12,8},{16,12},{20,16},{24,20},{28,24},{0,28},{5,1},{9... | collective-permute-start | bytes 3145736 | tf_op jit(solution)/shard_map/ppermute | solution.py:26
  219.1 6.5 %copy-start.10 = (bf16[1,512,32,64]{1,3,2,0:T(8,128)(2,1)S(1)}, bf16[1,512,32,64]{1,3,2,0:T(8,128)(2,1)}, u32[]{:S(2)}) copy-start(bf16[1,512,32,64]{1,3,2,0:T(8,128)(2,1)} %get-tuple-element.23) | copy-start | bytes 6291460
  219.1 6.5 %copy-start.22 = (f32[1536]{0:T(1024)S(1)}, f32[1536]{0:T(1024)}, u32[]{:S(2)}) copy-start(f32[1536]{0:T(1024)} %get-tuple-element.16) | copy-start | bytes 18436
  225.7 36.1 %collective-permute-start.17 = (bf16[256,1536]{1,0:T(8,128)(2,1)}, bf16[256,1536]{1,0:T(8,128)(2,1)}, u32[]{:S(2)}, u32[]{:S(2)}) collective-permute-start(bf16[256,1536]{1,0:T(8,128)(2,1)} %collective-permute-done.16), channel_id=1, source_target_pairs={{0,4},{4,8},{8,12},{12,16},{16,20},{20,24},{24,28},{28,0},{1,5},{5... | collective-permute-start | bytes 2359304 | tf_op jit(solution)/shard_map/ppermute | solution.py:24
  236.0 35.4 %copy-start.8 = (bf16[64,4,1536]{2,0,1:T(8,128)(2,1)S(1)}, bf16[64,4,1536]{2,0,1:T(8,128)(2,1)}, u32[]{:S(2)}) copy-start(bf16[64,4,1536]{2,0,1:T(8,128)(2,1)} %copy-done.7) | copy-start | bytes 2359300
  236.1 49.4 %collective-permute-start.20 = (bf16[256,1536]{1,0:T(8,128)(2,1)}, bf16[256,1536]{1,0:T(8,128)(2,1)}, u32[]{:S(2)}, u32[]{:S(2)}) collective-permute-start(bf16[256,1536]{1,0:T(8,128)(2,1)} %copy-done.12), channel_id=1, source_target_pairs={{4,0},{8,4},{12,8},{16,12},{20,16},{24,20},{28,24},{0,28},{5,1},{9... | collective-permute-start | bytes 2359304 | tf_op jit(solution)/shard_map/ppermute | solution.py:26
  238.4 49.1 %collective-permute-start.9 = (bf16[256,2048]{1,0:T(8,128)(2,1)}, bf16[256,2048]{1,0:T(8,128)(2,1)}, u32[]{:S(2)}, u32[]{:S(2)}) collective-permute-start(bf16[256,2048]{1,0:T(8,128)(2,1)} %collective-permute-done.8), channel_id=1, source_target_pairs={{0,4},{4,8},{8,12},{12,16},{16,20},{20,24},{24,28},{28,0},{1,5},{5... | collective-permute-start | bytes 3145736 | tf_op jit(solution)/shard_map/ppermute | solution.py:24
  239.3 98.4 %collective-permute-start.13 = (bf16[256,2048]{1,0:T(8,128)(2,1)}, bf16[256,2048]{1,0:T(8,128)(2,1)}, u32[]{:S(2)}, u32[]{:S(2)}) collective-permute-start(bf16[256,2048]{1,0:T(8,128)(2,1)} %collective-permute-done.12), channel_id=1, source_target_pairs={{4,0},{8,4},{12,8},{16,12},{20,16},{24,20},{28,24},{0,28},{5,1},{9... | collective-permute-start | bytes 3145736 | tf_op jit(solution)/shard_map/ppermute | solution.py:26
  260.9 45.6 %collective-permute-start.23 = (bf16[256,2048]{1,0:T(8,128)(2,1)}, bf16[256,2048]{1,0:T(8,128)(2,1)}, u32[]{:S(2)}, u32[]{:S(2)}) collective-permute-start(bf16[256,2048]{1,0:T(8,128)(2,1)} %collective-permute-done.22), channel_id=1, source_target_pairs={{0,4},{4,8},{8,12},{12,16},{16,20},{20,24},{24,28},{28,0},{1,5},{5... | collective-permute-start | bytes 3145736 | tf_op jit(solution)/shard_map/ppermute | solution.py:24
  261.8 160.4 %collective-permute-start.27 = (bf16[256,2048]{1,0:T(8,128)(2,1)}, bf16[256,2048]{1,0:T(8,128)(2,1)}, u32[]{:S(2)}, u32[]{:S(2)}) collective-permute-start(bf16[256,2048]{1,0:T(8,128)(2,1)} %collective-permute-done.26), channel_id=1, source_target_pairs={{4,0},{8,4},{12,8},{16,12},{20,16},{24,20},{28,24},{0,28},{5,1},{9... | collective-permute-start | bytes 3145736 | tf_op jit(solution)/shard_map/ppermute | solution.py:26
  287.5 35.1 %collective-permute-start.10 = (bf16[256,2048]{1,0:T(8,128)(2,1)}, bf16[256,2048]{1,0:T(8,128)(2,1)}, u32[]{:S(2)}, u32[]{:S(2)}) collective-permute-start(bf16[256,2048]{1,0:T(8,128)(2,1)} %collective-permute-done.9), channel_id=1, source_target_pairs={{0,4},{4,8},{8,12},{12,16},{16,20},{20,24},{24,28},{28,0},{1,5},{5... | collective-permute-start | bytes 3145736 | tf_op jit(solution)/shard_map/ppermute | solution.py:24
  306.5 25.5 %copy-start.6 = (bf16[64,4,2048]{2,0,1:T(8,128)(2,1)S(1)}, bf16[64,4,2048]{2,0,1:T(8,128)(2,1)}, u32[]{:S(2)}) copy-start(bf16[64,4,2048]{2,0,1:T(8,128)(2,1)} %copy-done.5) | copy-start | bytes 3145732
  306.5 77.7 %collective-permute-start.24 = (bf16[256,2048]{1,0:T(8,128)(2,1)}, bf16[256,2048]{1,0:T(8,128)(2,1)S(1)}, u32[]{:S(2)}, u32[]{:S(2)}) collective-permute-start(bf16[256,2048]{1,0:T(8,128)(2,1)} %collective-permute-done.23), channel_id=1, source_target_pairs={{0,4},{4,8},{8,12},{12,16},{16,20},{20,24},{24,28},{28,0},{1,5},{5... | collective-permute-start | bytes 3145736 | tf_op jit(solution)/shard_map/ppermute | solution.py:24
  340.0 8.6 %copy-start.9 = (bf16[1,512,32,64]{1,3,2,0:T(8,128)(2,1)S(1)}, bf16[1,512,32,64]{1,3,2,0:T(8,128)(2,1)}, u32[]{:S(2)}) copy-start(bf16[1,512,32,64]{1,3,2,0:T(8,128)(2,1)} %get-tuple-element.24) | copy-start | bytes 6291460
  340.0 8.6 %copy-start.24 = (f32[1,2048]{1,0:T(1,128)S(1)}, f32[1,2048]{1,0:T(1,128)}, u32[]{:S(2)}) copy-start(f32[1,2048]{1,0:T(1,128)} %get-tuple-element.42) | copy-start | bytes 24580
  380.0 29.3 %all-to-all-start.3 = ((bf16[4,512,512]{2,1,0:T(8,128)(2,1)}), bf16[4,512,512]{2,1,0:T(8,128)(2,1)S(1)}, u32[]{:S(2)}, u32[]{:S(2)}) async-start(bf16[4,512,512]{2,1,0:T(8,128)(2,1)} %bitcast.251), calls=%async_computation.3 | async-start | bytes 4194304 | tf_op jit(solution)/shard_map/all_to_all | solution.py:88
  387.6 22.1 %copy-start.11 = (bf16[1,512,512]{2,1,0:T(8,128)(2,1)S(1)}, bf16[1,512,512]{2,1,0:T(8,128)(2,1)}, u32[]{:S(2)}) copy-start(bf16[1,512,512]{2,1,0:T(8,128)(2,1)} %param.16) | copy-start | bytes 1572868
  387.6 22.1 %copy-start.20 = (f32[1,512]{1,0:T(1,128)S(1)}, f32[1,512]{1,0:T(1,128)}, u32[]{:S(2)}) copy-start(f32[1,512]{1,0:T(1,128)} %get-tuple-element.44) | copy-start | bytes 6148
  409.9 1.7 copy-start.3
  411.6 29.8 %all-to-all-start.4 = ((bf16[4,512,512]{1,2,0:T(8,128)(2,1)}), bf16[4,512,512]{1,2,0:T(8,128)(2,1)S(1)}, u32[]{:S(2)}, u32[]{:S(2)}) async-start(bf16[4,512,512]{1,2,0:T(8,128)(2,1)} %broadcast_in_dim.52), calls=%async_computation.4 | async-start | bytes 4194304 | tf_op jit(solution)/shard_map/all_to_all | solution.py:88
  441.4 1.4 copy-start.1
  445.8 3.7 copy-start.21
  466.8 5.5 %copy-start.2 = (f32[1,512,2,1,256]{4,1,2,3,0:T(8,128)S(1)}, f32[1,512,2,1,256]{4,1,2,3,0:T(8,128)}, u32[]{:S(2)}) copy-start(f32[1,512,2,1,256]{4,1,2,3,0:T(8,128)} %copy.74) | copy-start | bytes 3145732
  477.7 2.9 copy-start.23
  480.5 26.3 %copy-start.13 = (bf16[2,256,512]{2,1,0:T(8,128)(2,1)S(1)}, bf16[2,256,512]{2,1,0:T(8,128)(2,1)}, u32[]{:S(2)}) copy-start(bf16[2,256,512]{2,1,0:T(8,128)(2,1)} %convolution_convert_fusion) | copy-start | bytes 1572868
  511.1 28.8 %copy-start.4 = (bf16[1,512,512]{2,1,0:T(8,128)(2,1)S(1)}, bf16[1,512,512]{2,1,0:T(8,128)(2,1)}, u32[]{:S(2)}) copy-start(bf16[1,512,512]{2,1,0:T(8,128)(2,1)} %copy-done.3) | copy-start | bytes 1572868
  511.1 28.8 %copy-start.19 = (f32[1,512]{1,0:T(1,128)S(1)}, f32[1,512]{1,0:T(1,128)}, u32[]{:S(2)}) copy-start(f32[1,512]{1,0:T(1,128)} %get-tuple-element.43) | copy-start | bytes 6148
